TPU v7x, 256 devices: a whole 4x4x8 slice. The times are simulated.
256 devices in a mesh: dp: 16 (over x, y_hi, core), mp: 16 (over y_lo, z).
Axes of the slice: x: 4, y: 4 (y_hi: 2, y_lo: 2; y = y_hi * 2 + y_lo), z: 8, core: 2. Of those that a mesh axis runs over, the one named last changes fastest.
Arguments:
- tokens: bfloat16 [4096, 4096], P('dp'), may hold values from -32 to 32
- weights: bfloat16 [4096, 2, 3, 4096], P('dp', None, None, 'mp'), may hold values from -1 to 1
- block_modality: int32 [32], replicated, may hold values from 0 to 1
- doc_ids: int32 [4096], replicated, may hold values from 0 to 31, never falling along the last dimension, each value on 1 to 1024 neighbouring positions
- grad_out: bfloat16 [4096, 4096], P('dp', 'mp'), may hold values from -6 to 6
Outputs:
- attended: bfloat16 [4096, 4096], P('dp', 'mp')
- grad_tokens: bfloat16 [4096, 4096], P('dp', 'mp')
- grad_weights: bfloat16 [4096, 2, 3, 4096], P('dp', None, None, 'mp')
Inputs may be any that keep to these rules, and one draw needn't show every extreme that they name: doc_ids never falls along the sequence; a document is a run of equal ids of at most 1024 tokens, and one document has exactly 1024.
All inputs are finite; a program needn't handle non-finite values.
Results may differ from a plain program's by a relative error of at most 0.025.
Values may be sent and summed in bfloat16 or wider, within the bound.
No kernel may reach another device: no remote copies, remote signals or barrier semaphores. Data moves between devices by JAX's collectives and lax.ppermute only.
A program may use at most 128 MiB of HBM per device.

v0:
```python
import jax
import jax.numpy as jnp
from jax import lax
from jax.sharding import PartitionSpec as P

HD = 128
BLOCK = 128
SPAN = 4


def shifted(block, axis, distance):
    devices = range(lax.axis_size(axis))
    route = [(i - distance, i) for i in devices if i - distance in devices]
    return lax.ppermute(block, axis, route)


def select_product(block_rows, modality, text_mat, image_mat, contract):
    contraction = (((1,), (contract,)), ((), ()))
    return lax.cond(
        modality == 0,
        lambda: lax.dot_general(
            block_rows, text_mat, contraction, preferred_element_type=jnp.float32
        ),
        lambda: lax.dot_general(
            block_rows, image_mat, contraction, preferred_element_type=jnp.float32
        ),
    )


def blockwise(row_data, modalities, text_mat, image_mat, contract):
    blocks = row_data.reshape(modalities.shape[0], BLOCK, row_data.shape[1])

    def one_block(block_pair):
        return select_product(block_pair[0], block_pair[1], text_mat, image_mat, contract)

    result = lax.map(one_block, (blocks, modalities))
    return result.reshape(row_data.shape[0], result.shape[2])


def on_device(tokens, weights, block_modality, doc_ids, grad_out):
    local_rows = tokens.shape[0]
    width_rows = weights.shape[0]
    head_width = weights.shape[3]
    head_count = head_width // HD
    dp_devices = lax.axis_size("dp")
    local_blocks = local_rows // BLOCK
    front_pad = SPAN * local_rows
    window_len = front_pad + local_rows
    my_index = lax.axis_index("dp")
    scale_factor = HD ** (-0.5)
    my_mods = lax.dynamic_slice_in_dim(block_modality, my_index * local_blocks, local_blocks, 0)
    flat_weights = weights.reshape(width_rows, 2, 3 * head_width)
    text_local = flat_weights[:, 0]
    image_local = flat_weights[:, 1]
    columns = lax.all_to_all(tokens, "dp", split_axis=1, concat_axis=0, tiled=True)
    text_whole, image_whole = (
        lax.all_gather(text_local, "dp", axis=0, tiled=True),
        lax.all_gather(image_local, "dp", axis=0, tiled=True),
    )
    summed = blockwise(tokens, my_mods, text_whole, image_whole, 0)
    qkv = summed.astype(jnp.bfloat16).reshape(local_rows, 3, head_count, HD)
    queries = qkv[:, 0]
    key_values = qkv[:, 1:]
    received = []
    for distance in range(SPAN, 0, -1):
        received.append(shifted(key_values, "dp", distance))
    window = jnp.concatenate(received + [key_values], 0)
    key_rows = window[:, 0]
    value_rows = window[:, 1]
    docs_pad = jnp.concatenate([jnp.full((front_pad,), -1, jnp.int32), doc_ids], 0)
    key_docs = lax.dynamic_slice_in_dim(docs_pad, my_index * local_rows, window_len, 0)
    query_docs = lax.dynamic_slice_in_dim(doc_ids, my_index * local_rows, local_rows, 0)
    offsets = jnp.arange(window_len, dtype=jnp.int32) - front_pad
    allowed = (key_docs[None, :] == query_docs[:, None]) & (
        offsets[None, :] <= jnp.arange(local_rows, dtype=jnp.int32)[:, None]
    )
    scores = (
        jnp.einsum("qhd,khd->hqk", queries, key_rows, preferred_element_type=jnp.float32)
        * scale_factor
    )
    scores = jnp.where(allowed[None], scores, -1e30)
    top_score = jnp.max(scores, axis=-1, keepdims=True)
    expos = jnp.where(allowed[None], jnp.exp(scores - top_score), 0.0)
    probs_f = expos / jnp.sum(expos, axis=-1, keepdims=True)
    probs = probs_f.astype(jnp.bfloat16)
    attended = jnp.einsum("hqk,khd->qhd", probs, value_rows, preferred_element_type=jnp.float32)
    attended = attended.astype(jnp.bfloat16).reshape(local_rows, head_width)
    upstream = grad_out.reshape(local_rows, head_count, HD)
    dprob = jnp.einsum("qhd,khd->hqk", upstream, value_rows, preferred_element_type=jnp.float32)
    row_delta = jnp.sum(probs_f * dprob, axis=-1, keepdims=True)
    dscore = (probs_f * (dprob - row_delta)).astype(jnp.bfloat16)
    grad_q = (
        jnp.einsum("hqk,khd->qhd", dscore, key_rows, preferred_element_type=jnp.float32)
        * scale_factor
    )
    grad_k = (
        jnp.einsum("hqk,qhd->khd", dscore, queries, preferred_element_type=jnp.float32)
        * scale_factor
    )
    grad_v = jnp.einsum("hqk,qhd->khd", probs, upstream, preferred_element_type=jnp.float32)
    window_grads = jnp.stack([grad_k, grad_v], 1)
    own_grads = window_grads[front_pad:]
    for distance in range(1, SPAN + 1):
        lower_edge = front_pad - distance * local_rows
        sent_block = window_grads[lower_edge : lower_edge + local_rows]
        own_grads = own_grads + shifted(sent_block.astype(jnp.bfloat16), "dp", -distance).astype(
            sent_block.dtype
        )
    dqkv = (
        jnp.concatenate([grad_q[:, None], own_grads], 1)
        .astype(jnp.bfloat16)
        .reshape(local_rows, 3 * head_width)
    )
    gathered = lax.all_gather(dqkv, "dp", axis=0, tiled=True)
    column_groups = columns.reshape(dp_devices, local_blocks, BLOCK, width_rows)
    grad_groups = gathered.reshape(dp_devices, local_blocks, BLOCK, 3 * head_width)
    modality_groups = block_modality.reshape(dp_devices, local_blocks)
    modality_range = jnp.arange(2, dtype=jnp.int32)

    def accumulate(running, triple):
        column_group, grad_group, group_mods = triple
        per_block = jnp.einsum(
            "bnf,bnc->bfc", column_group, grad_group, preferred_element_type=jnp.float32
        )
        selector = (group_mods[:, None] == modality_range[None, :]).astype(jnp.float32)
        return (running + jnp.sum(selector[:, :, None, None] * per_block[:, None], axis=0), None)

    weight_sum, unused = lax.scan(
        accumulate,
        jnp.zeros((2, width_rows, 3 * head_width), jnp.float32),
        (column_groups, grad_groups, modality_groups),
    )
    grad_weights = (
        jnp.transpose(weight_sum, (1, 0, 2))
        .astype(jnp.bfloat16)
        .reshape(width_rows, 2, 3, head_width)
    )
    input_terms = blockwise(dqkv, my_mods, text_whole, image_whole, 1)
    grad_tokens = lax.psum_scatter(
        input_terms.astype(jnp.bfloat16), "mp", scatter_dimension=1, tiled=True
    )
    return (attended, grad_tokens, grad_weights)


def solution(mesh):
    return jax.shard_map(
        on_device,
        mesh=mesh,
        in_specs=(P("dp", None), P("dp", None, None, "mp"), P(), P(), P("dp", "mp")),
        out_specs=(P("dp", "mp"), P("dp", "mp"), P("dp", None, None, "mp")),
        check_vma=False,
    )
```

profile of v0, /device:TPU:4, one launch (start us, length us, event | category | flops | bytes accessed | tf_op | source)
XLA Modules:
  0.0 415.7 jit_solution(13535835044259661621)
XLA Ops:
  11.5 74.8 %all-gather.8.cloned.1.call-done = bf16[4096,1,768]{0,2,1:T(8,128)(2,1)} async-done(((bf16[256,1,768]{0,2,1:T(8,128)(2,1)}), bf16[4096,1,768]{0,2,1:T(8,128)(2,1)}) %all-gather.8.cloned.1.call-update) | async-done | bytes 6291472 | tf_op jit(solution)/shard_map/all_gather | solution.py:58
  86.4 8.6 %copy.59 = bf16[4096,768]{1,0:T(8,128)(2,1)} copy(bf16[4096,768]{0,1:T(8,128)(2,1)} %bitcast.114) | data formatting | bytes 12582912 | tf_op jit(solution)/shard_map/while | solution.py:36
  95.0 67.1 %all-gather.10.cloned.1.call-done = bf16[4096,1,768]{0,2,1:T(8,128)(2,1)} async-done(((bf16[256,1,768]{0,2,1:T(8,128)(2,1)}), bf16[4096,1,768]{0,2,1:T(8,128)(2,1)}) %all-gather.10.cloned.1.call-update) | async-done | bytes 6291472 | tf_op jit(solution)/shard_map/all_gather | solution.py:57
  162.1 8.8 %copy.60 = bf16[4096,768]{1,0:T(8,128)(2,1)} copy(bf16[4096,768]{0,1:T(8,128)(2,1)} %bitcast.115) | data formatting | bytes 12582912 | tf_op jit(solution)/shard_map/while | solution.py:36
  170.9 11.7 %while.31 = (s32[]{:T(128)}, bf16[2,128,768]{2,1,0:T(8,128)(2,1)}, s32[2]{0:T(128)S(1)}, bf16[2,128,4096]{2,1,0:T(8,128)(2,1)S(1)}, bf16[4096,768]{1,0:T(8,128)(...) while((s32[]{:T(128)}, bf16[2,128,768]{2,1,0:T(8,128)(2,1)}, s32[2]{0:T(128)S(1)}, ...), condition=%wide.region_3.4_spmd, body=%wide.region_0.3_spmd.sunk | while | flops 805306368 | bytes 10027175 | solution.py:36
  172.2 3.8 conditional.4
  172.3 3.8 convolution_bitcast_fusion.1
  178.1 3.8 conditional.4
  178.1 3.8 convolution_bitcast_fusion.1
  183.9 4.3 %collective-permute-start = (bf16[256,2,2,128]{3,0,2,1:T(8,128)(2,1)S(1)}, bf16[256,2,2,128]{3,0,2,1:T(8,128)(2,1)}, u32[]{:S(2)}, u32[]{:S(2)}) collective-permute-start(bf16[256,2,2,128]{3,0,2,1:T(8,128)(2,1)S(1)} %copy.84), channel_id=1, source_target_pairs={{0,64},{16,80},{32,96},{48,112},{64,128},{80,144},{96,160},{112,17... | collective-permute-start | bytes 786440 | tf_op jit(solution)/shard_map/ppermute | solution.py:14
  190.3 4.0 collective-permute-start.2
  200.8 6.3 %collective-permute-done.2 = bf16[256,2,2,128]{3,0,2,1:T(8,128)(2,1)} collective-permute-done((bf16[256,2,2,128]{3,0,2,1:T(8,128)(2,1)S(1)}, bf16[256,2,2,128]{3,0,2,1:T(8,128)(2,1)}, u32[]{:S(2)}, u32[]{:S(2)}) %collective-permute-start.2) | collective-permute-done | bytes 262176 | tf_op jit(solution)/shard_map/ppermute | solution.py:14
  210.3 4.0 fusion.30
  214.3 2.7 multiply_reduce_fusion.1
  218.6 3.4 collective-permute-start.7
  225.9 4.6 %collective-permute-start.4 = (bf16[256,2,2,128]{0,3,2,1:T(8,128)(2,1)S(1)}, bf16[256,2,2,128]{0,3,2,1:T(8,128)(2,1)S(1)}, u32[]{:S(2)}, u32[]{:S(2)}) collective-permute-start(bf16[256,2,2,128]{0,3,2,1:T(8,128)(2,1)S(1)} %get-tuple-element.257), channel_id=1, source_target_pairs={{16,0},{32,16},{48,32},{64,48},{80,64},{96,80},{112,96},{128,112},... | collective-permute-start | bytes 786440 | tf_op jit(solution)/shard_map/ppermute | solution.py:14
  234.4 3.0 collective-permute-done.5
  237.4 2.8 collective-permute-done.4
  241.2 2.5 copy.72
  243.7 7.3 %all-to-all-start = ((bf16[256,16,256]{0,2,1:T(8,128)(2,1)}), bf16[256,16,256]{0,2,1:T(8,128)(2,1)}, u32[]{:S(2)}, u32[]{:S(2)}) async-start(bf16[256,16,256]{0,2,1:T(8,128)(2,1)} %bitcast.113), calls=%async_computation.1 | async-start | bytes 4194304 | tf_op jit(solution)/shard_map/all_to_all | solution.py:55
  251.4 30.8 %all-to-all-done = bf16[256,16,256]{0,2,1:T(8,128)(2,1)} async-done(((bf16[256,16,256]{0,2,1:T(8,128)(2,1)}), bf16[256,16,256]{0,2,1:T(8,128)(2,1)}, u32[]{:S(2)}, u32[]{:S(2)}) %all-to-all-start) | async-done | bytes 2097184 | tf_op jit(solution)/shard_map/all_to_all | solution.py:55
  282.2 3.9 copy.73
  286.1 2.6 convolution_convert_fusion
  290.1 14.7 %while.32 = (s32[]{:T(128)}, bf16[2,128,4096]{2,1,0:T(8,128)(2,1)}, s32[2]{0:T(128)S(1)}, bf16[2,128,768]{2,1,0:T(8,128)(2,1)S(1)}, bf16[4096,768]{1,0:T(8,128)(...) while((s32[]{:T(128)}, bf16[2,128,4096]{2,1,0:T(8,128)(2,1)}, s32[2]{0:T(128)S(1)}, ...), condition=%wide.region_10.11_spmd, body=%wide.region_7.10_spmd.sunk | while | flops 805306368 | bytes 10027175 | solution.py:36
  291.3 4.9 %conditional.5 = (bf16[1,128,4096]{2,1,0:T(8,128)(2,1)S(1)}) conditional(s32[]{:T(128)} %bitcast.106, (bf16[128,768]{1,0:T(8,128)(2,1)S(1)}, bf16[4096,768]{1,0:T(8,128)(2,1)}) %tuple.94, (bf16[128,768]{1,0:T(8,128)(2,1)S(1)}, bf16[4096,768]{1,0:T(8,128)(2,1)}) %tuple.95), branch_computations={%region_8.8_spmd, %region_9.9_spmd} | conditional | flops 805306368 | bytes 7536648 | solution.py:19
  291.3 4.9 %convolution_bitcast_fusion.3 = bf16[1,128,4096]{2,1,0:T(8,128)(2,1)S(1)} fusion(bf16[128,768]{1,0:T(8,128)(2,1)S(1)} %get-tuple-element.109, bf16[4096,768]{1,0:T(8,128)(2,1)} %get-tuple-element.110), kind=kOutput, calls=%fused_computation.6 | convolution fusion | flops 805306368 | bytes 7536640 | tf_op jit(solution)/shard_map/while/body/eval_jaxpr/cond/branch_1_fun/dot_general | solution.py:21
  298.6 5.1 %conditional.5 = (bf16[1,128,4096]{2,1,0:T(8,128)(2,1)S(1)}) conditional(s32[]{:T(128)} %bitcast.106, (bf16[128,768]{1,0:T(8,128)(2,1)S(1)}, bf16[4096,768]{1,0:T(8,128)(2,1)}) %tuple.94, (bf16[128,768]{1,0:T(8,128)(2,1)S(1)}, bf16[4096,768]{1,0:T(8,128)(2,1)}) %tuple.95), branch_computations={%region_8.8_spmd, %region_9.9_spmd} | conditional | flops 805306368 | bytes 7536648 | solution.py:19
  298.6 5.1 %convolution_bitcast_fusion.3 = bf16[1,128,4096]{2,1,0:T(8,128)(2,1)S(1)} fusion(bf16[128,768]{1,0:T(8,128)(2,1)S(1)} %get-tuple-element.109, bf16[4096,768]{1,0:T(8,128)(2,1)} %get-tuple-element.110), kind=kOutput, calls=%fused_computation.6 | convolution fusion | flops 805306368 | bytes 7536640 | tf_op jit(solution)/shard_map/while/body/eval_jaxpr/cond/branch_1_fun/dot_general | solution.py:21
  304.8 26.7 %all-gather.6.cloned.1.call-done = bf16[4096,768]{0,1:T(8,128)(2,1)} async-done(((bf16[256,768]{0,1:T(8,128)(2,1)}), bf16[4096,768]{0,1:T(8,128)(2,1)}) %all-gather.6.cloned.1.call-update) | async-done | bytes 6291472 | tf_op jit(solution)/shard_map/all_gather | solution.py:114
  331.5 8.6 %copy.74 = bf16[4096,768]{1,0:T(8,128)(2,1)} copy(bf16[4096,768]{0,1:T(8,128)(2,1)} %all-gather.6.cloned.1.call-done) | data formatting | bytes 12582912 | tf_op jit(solution)/shard_map/all_gather | solution.py:114
  340.1 39.0 %while.33 = (s32[]{:T(128)}, f32[2,256,768]{2,1,0:T(8,128)S(1)}, s32[16,2]{1,0:T(8,128)S(1)}, bf16[16,2,128,256]{3,2,1,0:T(8,128)(2,1)}, bf16[16,2,128,768]{3,2,1,0:T(8,128)(2,1)}, /*index=5*/s32[]{:T(128)}, s32[]{:T(128)}) while((s32[]{:T(128)}, f32[2,256,768]{2,1,0:T(8,128)S(1)}, s32[16,2]{1,0:T(8,128)S(1)}, ...), condition=%wide.region_14.15_spmd.clone, body=%wide.region_12.14_spmd.clone.sunk | while | flops 102629384 | bytes 9962651 | solution.py:128
  381.3 27.9 %reduce-scatter.2.cloned.1.call-done = bf16[256,256]{1,0:T(8,128)(2,1)} async-done(((bf16[256,4096]{1,0:T(8,128)(2,1)}), bf16[256,256]{1,0:T(8,128)(2,1)}) %reduce-scatter.2.cloned.1.call-update) | async-done | bytes 131088 | tf_op jit(solution)/shard_map/reduce_scatter | solution.py:139
  (156 shorter events, 75.7 us)
Async XLA Ops:
  7.2 4.1 copy-start.6
  7.2 4.2 %copy-start.5 = (s32[4096]{0:T(1024)S(1)}, s32[4096]{0:T(1024)}, u32[]{:S(2)}) copy-start(s32[4096]{0:T(1024)} %param.18) | copy-start | bytes 49156
  7.2 79.2 %all-gather.8.cloned.1.call-start = ((), (), s32[]{:S(2)}) async-start(), calls=%async_computation.4 | async-start | bytes 6684672 | tf_op jit(solution)/shard_map/all_gather | solution.py:58
  10.5 151.6 %all-gather.10.cloned.1.call-start = ((), (), s32[]{:S(2)}) async-start(), calls=%async_computation.5 | async-start | bytes 6684672 | tf_op jit(solution)/shard_map/all_gather | solution.py:57
  11.2 320.3 %all-gather.6.cloned.1.call-start = ((), (), s32[]{:S(2)}) async-start(), calls=%async_computation.3 | async-start | bytes 6684672 | tf_op jit(solution)/shard_map/all_gather | solution.py:114
  162.1 8.8 %copy-start = (bf16[256,4096]{1,0:T(8,128)(2,1)S(1)}, bf16[256,4096]{1,0:T(8,128)(2,1)}, u32[]{:S(2)}) copy-start(bf16[256,4096]{1,0:T(8,128)(2,1)} %param.15) | copy-start | bytes 6291460
  182.6 12.0 %copy-start.3 = (bf16[256,256]{1,0:T(8,128)(2,1)S(1)}, bf16[256,256]{1,0:T(8,128)(2,1)}, u32[]{:S(2)}) copy-start(bf16[256,256]{1,0:T(8,128)(2,1)} %param.19) | copy-start | bytes 393220
  183.9 13.4 %collective-permute-start = (bf16[256,2,2,128]{3,0,2,1:T(8,128)(2,1)S(1)}, bf16[256,2,2,128]{3,0,2,1:T(8,128)(2,1)}, u32[]{:S(2)}, u32[]{:S(2)}) collective-permute-start(bf16[256,2,2,128]{3,0,2,1:T(8,128)(2,1)S(1)} %copy.84), channel_id=1, source_target_pairs={{0,64},{16,80},{32,96},{48,112},{64,128},{80,144},{96,160},{112,17... | collective-permute-start | bytes 786440 | tf_op jit(solution)/shard_map/ppermute | solution.py:14
  188.2 10.9 %collective-permute-start.1 = (bf16[256,2,2,128]{3,0,2,1:T(8,128)(2,1)S(1)}, bf16[256,2,2,128]{3,0,2,1:T(8,128)(2,1)}, u32[]{:S(2)}, u32[]{:S(2)}) collective-permute-start(bf16[256,2,2,128]{3,0,2,1:T(8,128)(2,1)S(1)} %copy.84), channel_id=1, source_target_pairs={{0,48},{16,64},{32,80},{48,96},{64,112},{80,128},{96,144},{112,160... | collective-permute-start | bytes 786440 | tf_op jit(solution)/shard_map/ppermute | solution.py:14
  190.3 16.8 %collective-permute-start.2 = (bf16[256,2,2,128]{3,0,2,1:T(8,128)(2,1)S(1)}, bf16[256,2,2,128]{3,0,2,1:T(8,128)(2,1)}, u32[]{:S(2)}, u32[]{:S(2)}) collective-permute-start(bf16[256,2,2,128]{3,0,2,1:T(8,128)(2,1)S(1)} %copy.84), channel_id=1, source_target_pairs={{0,32},{16,48},{32,64},{48,80},{64,96},{80,112},{96,128},{112,144}... | collective-permute-start | bytes 786440 | tf_op jit(solution)/shard_map/ppermute | solution.py:14
  195.4 13.4 %collective-permute-start.3 = (bf16[256,2,2,128]{3,0,2,1:T(8,128)(2,1)S(1)}, bf16[256,2,2,128]{3,0,2,1:T(8,128)(2,1)S(1)}, u32[]{:S(2)}, u32[]{:S(2)}) collective-permute-start(bf16[256,2,2,128]{3,0,2,1:T(8,128)(2,1)S(1)} %copy.84), channel_id=1, source_target_pairs={{0,16},{16,32},{32,48},{48,64},{64,80},{80,96},{96,112},{112,128},... | collective-permute-start | bytes 786440 | tf_op jit(solution)/shard_map/ppermute | solution.py:14
  210.3 4.0 copy-start.4
  214.3 2.7 copy-start.2
  218.6 13.5 %collective-permute-start.7 = (bf16[256,2,2,128]{0,3,2,1:T(8,128)(2,1)S(1)}, bf16[256,2,2,128]{0,3,2,1:T(8,128)(2,1)S(1)}, u32[]{:S(2)}, u32[]{:S(2)}) collective-permute-start(bf16[256,2,2,128]{0,3,2,1:T(8,128)(2,1)S(1)} %get-tuple-element.258), channel_id=1, source_target_pairs={{64,0},{80,16},{96,32},{112,48},{128,64},{144,80},{160,96},{176,11... | collective-permute-start | bytes 786440 | tf_op jit(solution)/shard_map/ppermute | solution.py:14
  222.0 12.4 %collective-permute-start.6 = (bf16[256,2,2,128]{0,3,2,1:T(8,128)(2,1)S(1)}, bf16[256,2,2,128]{0,3,2,1:T(8,128)(2,1)S(1)}, u32[]{:S(2)}, u32[]{:S(2)}) collective-permute-start(bf16[256,2,2,128]{0,3,2,1:T(8,128)(2,1)S(1)} %get-tuple-element.259), channel_id=1, source_target_pairs={{48,0},{64,16},{80,32},{96,48},{112,64},{128,80},{144,96},{160,112... | collective-permute-start | bytes 786440 | tf_op jit(solution)/shard_map/ppermute | solution.py:14
  223.9 13.4 %collective-permute-start.5 = (bf16[256,2,2,128]{0,3,2,1:T(8,128)(2,1)S(1)}, bf16[256,2,2,128]{0,3,2,1:T(8,128)(2,1)S(1)}, u32[]{:S(2)}, u32[]{:S(2)}) collective-permute-start(bf16[256,2,2,128]{0,3,2,1:T(8,128)(2,1)S(1)} %get-tuple-element.260), channel_id=1, source_target_pairs={{32,0},{48,16},{64,32},{80,48},{96,64},{112,80},{128,96},{144,112}... | collective-permute-start | bytes 786440 | tf_op jit(solution)/shard_map/ppermute | solution.py:14
  225.9 14.3 %collective-permute-start.4 = (bf16[256,2,2,128]{0,3,2,1:T(8,128)(2,1)S(1)}, bf16[256,2,2,128]{0,3,2,1:T(8,128)(2,1)S(1)}, u32[]{:S(2)}, u32[]{:S(2)}) collective-permute-start(bf16[256,2,2,128]{0,3,2,1:T(8,128)(2,1)S(1)} %get-tuple-element.257), channel_id=1, source_target_pairs={{16,0},{32,16},{48,32},{64,48},{80,64},{96,80},{112,96},{128,112},... | collective-permute-start | bytes 786440 | tf_op jit(solution)/shard_map/ppermute | solution.py:14
  243.7 38.5 %all-to-all-start = ((bf16[256,16,256]{0,2,1:T(8,128)(2,1)}), bf16[256,16,256]{0,2,1:T(8,128)(2,1)}, u32[]{:S(2)}, u32[]{:S(2)}) async-start(bf16[256,16,256]{0,2,1:T(8,128)(2,1)} %bitcast.113), calls=%async_computation.1 | async-start | bytes 4194304 | tf_op jit(solution)/shard_map/all_to_all | solution.py:55
  251.0 158.1 %reduce-scatter.2.cloned.1.call-start = ((), (), s32[]{:S(2)}) async-start(), calls=%async_computation.2 | async-start | bytes 2228224 | tf_op jit(solution)/shard_map/reduce_scatter | solution.py:139
  286.1 3.4 copy-start.1
Sparse Core Ops, SparseCore 0:
  10.6 75.7 all-gather.7
  88.9 73.1 all-gather.9
  241.3 90.1 all-gather.5
  334.5 74.6 reduce-scatter.1
where the time goes:
time: 417 us; the launch traced here: 416 us
  waiting for transfers between devices  242 us (58%)
  local copies, waits for them, and re-layouts  54.6 us (13%)
  matrix products  53 us (13%)
  starting transfers between devices  31.7 us (8%)
  other arithmetic  16.4 us (4%)
  between operations  14 us (3%)
    all_gather x1, waiting for transfers between devices, on_device(): lax.all_gather(image_local, 'dp', axis=0, tiled=True)  74.8 us
    all_gather x1, waiting for transfers between devices, on_device(): lax.all_gather(text_local, 'dp', axis=0, tiled=True)  67.1 us
    all_to_all x1, waiting for transfers between devices, on_device(): lax.all_to_all(tokens, 'dp', split_axis=1, concat_axis=0, tiled=True)  30.8 us
    reduce_scatter x1, waiting for transfers between devices, on_device(): lax.psum_scatter(input_terms.astype(jnp.bfloat16), 'mp', scatter_dimensio...  27.9 us
    all_gather x1, waiting for transfers between devices, on_device(): gathered = lax.all_gather(dqkv, 'dp', axis=0, tiled=True)  26.7 us
    ppermute x8, starting transfers between devices, shifted(): return lax.ppermute(block, axis, route)  24.1 us
    dot_general x16, matrix products, accumulate(): jnp.einsum('bnf,bnc->bfc', column_group, grad_group, preferred_element_ty...  23.6 us
    while x3, local copies, waits for them, and re-layouts, blockwise(): result = lax.map(one_block, (blocks, modalities))  17.9 us
  transfers between devices with their start and end apart: 13, of which 9 were waited for; matrix products, arithmetic and copies ran while one was open for 22% of the time, Pallas kernels for 0%

commit v1 on v0

--- a/solution.py
+++ b/solution.py
@@ -55,7 +55,9 @@
     columns = lax.all_to_all(tokens, "dp", split_axis=1, concat_axis=0, tiled=True)
     text_whole, image_whole = (
         lax.all_gather(text_local, "dp", axis=0, tiled=True),
-        lax.all_gather(image_local, "dp", axis=0, tiled=True),
+        jnp.concatenate(
+            lax.all_to_all(jnp.stack([image_local] * lax.axis_size("dp")), "dp", 0, 0), axis=0
+        ),
     )
     summed = blockwise(tokens, my_mods, text_whole, image_whole, 0)
     qkv = summed.astype(jnp.bfloat16).reshape(local_rows, 3, head_count, HD)

time: 417 us -> 389 us (0.933)
  waiting for transfers between devices: 242 us -> 212 us
  starting transfers between devices: 31.7 us -> 41.2 us
  local copies, waits for them, and re-layouts: 54.6 us -> 47.7 us
    all_gather x1 -> x0, waiting for transfers between devices: 74.8 us -> none  [on_device(): lax.all_gather(image_local, 'dp', axis=0, tiled=True)]
    all_gather x1, waiting for transfers between devices: 67.1 us -> 112 us  [on_device(): lax.all_gather(text_local, 'dp', axis=0, tiled=True)]
    while x3 -> x2, local copies, waits for them, and re-layouts: 17.9 us -> 9.2 us  [blockwise(): result = lax.map(one_block, (blocks, modalities))]
    all_to_all x0 -> x1, starting transfers between devices: none -> 7.58 us  [on_device(): lax.all_to_all(jnp.stack([image_local] * lax.axis_size('dp')), 'dp', 0, 0)]
    unnamed x23 -> x21, local copies, waits for them, and re-layouts: 13.3 us -> 13.3 us
  transfers between devices with their start and end apart: 13 -> 13, of which waited for: 9 -> 9; matrix products, arithmetic and copies ran while one was open for 22% -> 24% of each run, Pallas kernels for 0% -> 0%
where the time goes in v1:
time: 389 us; the launch traced here: 388 us
  waiting for transfers between devices  212 us (54%)
  matrix products  53 us (14%)
  local copies, waits for them, and re-layouts  47.7 us (12%)
  starting transfers between devices  41.2 us (11%)
  other arithmetic  16.4 us (4%)
  between operations  14 us (4%)
    all_gather x1, waiting for transfers between devices, on_device(): lax.all_gather(text_local, 'dp', axis=0, tiled=True)  112 us
    all_to_all x1, waiting for transfers between devices, on_device(): lax.all_to_all(tokens, 'dp', split_axis=1, concat_axis=0, tiled=True)  30.8 us
    reduce_scatter x1, waiting for transfers between devices, on_device(): lax.psum_scatter(input_terms.astype(jnp.bfloat16), 'mp', scatter_dimensio...  28.1 us
    all_gather x1, waiting for transfers between devices, on_device(): gathered = lax.all_gather(dqkv, 'dp', axis=0, tiled=True)  26.5 us
    ppermute x8, starting transfers between devices, shifted(): return lax.ppermute(block, axis, route)  25.6 us
    dot_general x16, matrix products, accumulate(): jnp.einsum('bnf,bnc->bfc', column_group, grad_group, preferred_element_ty...  23.6 us
    dot_general x4, matrix products, select_product(): lax.dot_general(block_rows, text_mat, contraction, preferred_element_type...  17.6 us
    ppermute x8, waiting for transfers between devices, shifted(): return lax.ppermute(block, axis, route)  14.9 us
  transfers between devices with their start and end apart: 13, of which 9 were waited for; matrix products, arithmetic and copies ran while one was open for 24% of the time, Pallas kernels for 0%

profile of v1, /device:TPU:4, one launch (start us, length us, event | category | flops | bytes accessed | tf_op | source)
XLA Modules:
  0.0 387.8 jit_solution(2169783686246915007)
XLA Ops:
  10.5 3.3 stack.12
  13.7 7.6 %all-to-all-start = ((bf16[16,256,768]{2,1,0:T(8,128)(2,1)}), bf16[16,256,768]{2,1,0:T(8,128)(2,1)}, u32[]{:S(2)}, u32[]{:S(2)}) async-start(bf16[16,256,768]{2,1,0:T(8,128)(2,1)} %stack.12), calls=%async_computation | async-start | bytes 12582912 | tf_op jit(solution)/shard_map/all_to_all | solution.py:59
  21.6 111.6 %all-gather.6.cloned.1.call-done = bf16[4096,1,768]{0,2,1:T(8,128)(2,1)} async-done(((bf16[256,1,768]{0,2,1:T(8,128)(2,1)}), bf16[4096,1,768]{0,2,1:T(8,128)(2,1)}) %all-gather.6.cloned.1.call-update) | async-done | bytes 6291472 | tf_op jit(solution)/shard_map/all_gather | solution.py:57
  133.2 8.8 %copy.58 = bf16[4096,768]{1,0:T(8,128)(2,1)} copy(bf16[4096,768]{0,1:T(8,128)(2,1)} %bitcast.116) | data formatting | bytes 12582912 | tf_op jit(solution)/shard_map/while | solution.py:36
  142.0 10.4 %while.31 = (s32[]{:T(128)}, bf16[2,128,768]{2,1,0:T(8,128)(2,1)S(1)}, s32[2]{0:T(128)S(1)}, bf16[2,128,4096]{2,1,0:T(8,128)(2,1)S(1)}, bf16[4096,768]{1,0:T(8,1...) while((s32[]{:T(128)}, bf16[2,128,768]{2,1,0:T(8,128)(2,1)S(1)}, s32[2]{0:T(128)S(1)}, ...), condition=%wide.region_3.4_spmd, body=%wide.region_0.3_spmd.sunk | while | flops 805306368 | bytes 10027175 | solution.py:36
  143.3 3.8 conditional.4
  143.3 3.8 convolution_bitcast_fusion.1
  148.5 3.8 conditional.4
  148.6 3.8 convolution_bitcast_fusion.1
  152.8 2.6 collective-permute-start
  155.4 6.6 %collective-permute-start.1 = (bf16[256,2,2,128]{3,0,2,1:T(8,128)(2,1)S(1)}, bf16[256,2,2,128]{3,0,2,1:T(8,128)(2,1)}, u32[]{:S(2)}, u32[]{:S(2)}) collective-permute-start(bf16[256,2,2,128]{3,0,2,1:T(8,128)(2,1)S(1)} %copy.81), channel_id=1, source_target_pairs={{0,48},{16,64},{32,80},{48,96},{64,112},{80,128},{96,144},{112,160... | collective-permute-start | bytes 786440 | tf_op jit(solution)/shard_map/ppermute | solution.py:14
  171.8 6.2 %collective-permute-done.2 = bf16[256,2,2,128]{3,0,2,1:T(8,128)(2,1)} collective-permute-done((bf16[256,2,2,128]{3,0,2,1:T(8,128)(2,1)S(1)}, bf16[256,2,2,128]{3,0,2,1:T(8,128)(2,1)}, u32[]{:S(2)}, u32[]{:S(2)}) %collective-permute-start.2) | collective-permute-done | bytes 262176 | tf_op jit(solution)/shard_map/ppermute | solution.py:14
  181.8 4.0 %fusion.30 = (f32[2,256]{1,0:T(2,128)S(1)}, f32[2,256,1280]{2,1,0:T(8,128)}) fusion(pred[256,1280]{1,0:T(8,128)(4,1)S(1)} %fusion.16, bf16[1280,2,2,128]{3,0,2,1:T(8,128)(2,1)} %constant_dynamic-update-slice_fusion.2, bf16[256,1,2,128]{3,2,1,0:T(2,128)(2,1)S(1)} %slice.52), kind=kOutput, calls=%fused_computation.66 | convolution fusion | flops 171050240 | bytes 4065280 | tf_op jit(solution)/shard_map/sub | solution.py:85
  185.8 2.7 multiply_reduce_fusion.1
  190.1 3.6 collective-permute-start.7
  197.6 4.6 %collective-permute-start.4 = (bf16[256,2,2,128]{0,3,2,1:T(8,128)(2,1)S(1)}, bf16[256,2,2,128]{0,3,2,1:T(8,128)(2,1)S(1)}, u32[]{:S(2)}, u32[]{:S(2)}) collective-permute-start(bf16[256,2,2,128]{0,3,2,1:T(8,128)(2,1)S(1)} %get-tuple-element.257), channel_id=1, source_target_pairs={{16,0},{32,16},{48,32},{64,48},{80,64},{96,80},{112,96},{128,112},... | collective-permute-start | bytes 786440 | tf_op jit(solution)/shard_map/ppermute | solution.py:14
  206.1 3.1 collective-permute-done.5
  209.2 2.8 collective-permute-done.4
  213.0 2.5 copy.69
  215.5 7.7 %all-to-all-start.1 = ((bf16[256,16,256]{0,2,1:T(8,128)(2,1)}), bf16[256,16,256]{0,2,1:T(8,128)(2,1)}, u32[]{:S(2)}, u32[]{:S(2)}) async-start(bf16[256,16,256]{0,2,1:T(8,128)(2,1)} %bitcast.115), calls=%async_computation.2 | async-start | bytes 4194304 | tf_op jit(solution)/shard_map/all_to_all | solution.py:55
  223.5 30.8 %all-to-all-done.1 = bf16[256,16,256]{0,2,1:T(8,128)(2,1)} async-done(((bf16[256,16,256]{0,2,1:T(8,128)(2,1)}), bf16[256,16,256]{0,2,1:T(8,128)(2,1)}, u32[]{:S(2)}, u32[]{:S(2)}) %all-to-all-start.1) | async-done | bytes 2097184 | tf_op jit(solution)/shard_map/all_to_all | solution.py:55
  254.3 3.9 %copy.70 = bf16[16,256,256]{2,1,0:T(8,128)(2,1)} copy(bf16[16,256,256]{1,2,0:T(8,128)(2,1)} %bitcast.27) | data formatting | bytes 4194304 | tf_op jit(solution)/shard_map/all_to_all | solution.py:55
  258.2 2.6 convolution_convert_fusion
  262.2 14.8 %while.32 = (s32[]{:T(128)}, bf16[2,128,4096]{2,1,0:T(8,128)(2,1)}, s32[2]{0:T(128)S(1)}, bf16[2,128,768]{2,1,0:T(8,128)(2,1)S(1)}, bf16[4096,768]{1,0:T(8,128)(...) while((s32[]{:T(128)}, bf16[2,128,4096]{2,1,0:T(8,128)(2,1)}, s32[2]{0:T(128)S(1)}, ...), condition=%wide.region_10.11_spmd, body=%wide.region_7.10_spmd.sunk | while | flops 805306368 | bytes 10027175 | solution.py:36
  263.5 4.9 %conditional.5 = (bf16[1,128,4096]{2,1,0:T(8,128)(2,1)S(1)}) conditional(s32[]{:T(128)} %bitcast.108, (bf16[128,768]{1,0:T(8,128)(2,1)S(1)}, bf16[4096,768]{1,0:T(8,128)(2,1)}) %tuple.94, (bf16[128,768]{1,0:T(8,128)(2,1)S(1)}, bf16[4096,768]{1,0:T(8,128)(2,1)}) %tuple.95), branch_computations={%region_8.8_spmd, %region_9.9_spmd} | conditional | flops 805306368 | bytes 7536648 | solution.py:19
  263.5 4.9 %convolution_bitcast_fusion.3 = bf16[1,128,4096]{2,1,0:T(8,128)(2,1)S(1)} fusion(bf16[128,768]{1,0:T(8,128)(2,1)S(1)} %get-tuple-element.109, bf16[4096,768]{1,0:T(8,128)(2,1)} %get-tuple-element.110), kind=kOutput, calls=%fused_computation.6 | convolution fusion | flops 805306368 | bytes 7536640 | tf_op jit(solution)/shard_map/while/body/eval_jaxpr/cond/branch_1_fun/dot_general | solution.py:21
  270.8 5.1 %conditional.5 = (bf16[1,128,4096]{2,1,0:T(8,128)(2,1)S(1)}) conditional(s32[]{:T(128)} %bitcast.108, (bf16[128,768]{1,0:T(8,128)(2,1)S(1)}, bf16[4096,768]{1,0:T(8,128)(2,1)}) %tuple.94, (bf16[128,768]{1,0:T(8,128)(2,1)S(1)}, bf16[4096,768]{1,0:T(8,128)(2,1)}) %tuple.95), branch_computations={%region_8.8_spmd, %region_9.9_spmd} | conditional | flops 805306368 | bytes 7536648 | solution.py:19
  270.8 5.0 %convolution_bitcast_fusion.3 = bf16[1,128,4096]{2,1,0:T(8,128)(2,1)S(1)} fusion(bf16[128,768]{1,0:T(8,128)(2,1)S(1)} %get-tuple-element.109, bf16[4096,768]{1,0:T(8,128)(2,1)} %get-tuple-element.110), kind=kOutput, calls=%fused_computation.6 | convolution fusion | flops 805306368 | bytes 7536640 | tf_op jit(solution)/shard_map/while/body/eval_jaxpr/cond/branch_1_fun/dot_general | solution.py:21
  277.0 26.5 %all-gather.4.cloned.1.call-done = bf16[4096,768]{0,1:T(8,128)(2,1)} async-done(((bf16[256,768]{0,1:T(8,128)(2,1)}), bf16[4096,768]{0,1:T(8,128)(2,1)}) %all-gather.4.cloned.1.call-update) | async-done | bytes 6291472 | tf_op jit(solution)/shard_map/all_gather | solution.py:116
  303.5 8.6 %copy.71 = bf16[4096,768]{1,0:T(8,128)(2,1)} copy(bf16[4096,768]{0,1:T(8,128)(2,1)} %all-gather.4.cloned.1.call-done) | data formatting | bytes 12582912 | tf_op jit(solution)/shard_map/all_gather | solution.py:116
  312.1 39.0 %while.33 = (s32[]{:T(128)}, f32[2,256,768]{2,1,0:T(8,128)S(1)}, s32[16,2]{1,0:T(8,128)S(1)}, bf16[16,2,128,256]{3,2,1,0:T(8,128)(2,1)}, bf16[16,2,128,768]{3,2,1,0:T(8,128)(2,1)}, /*index=5*/s32[]{:T(128)}, s32[]{:T(128)}) while((s32[]{:T(128)}, f32[2,256,768]{2,1,0:T(8,128)S(1)}, s32[16,2]{1,0:T(8,128)S(1)}, ...), condition=%wide.region_14.15_spmd.clone, body=%wide.region_12.14_spmd.clone.sunk | while | flops 102629384 | bytes 9962651 | solution.py:130
  353.2 28.1 %reduce-scatter.2.cloned.1.call-done = bf16[256,256]{1,0:T(8,128)(2,1)} async-done(((bf16[256,4096]{1,0:T(8,128)(2,1)}), bf16[256,256]{1,0:T(8,128)(2,1)}) %reduce-scatter.2.cloned.1.call-update) | async-done | bytes 131088 | tf_op jit(solution)/shard_map/reduce_scatter | solution.py:141
  (154 shorter events, 74.4 us)
Async XLA Ops:
  7.2 126.1 %all-gather.6.cloned.1.call-start = ((), (), s32[]{:S(2)}) async-start(), calls=%async_computation.5 | async-start | bytes 6684672 | tf_op jit(solution)/shard_map/all_gather | solution.py:57
  13.7 7.7 %copy-start.5 = (s32[32]{0:T(128)S(1)}, s32[32]{0:T(128)}, u32[]{:S(2)}) copy-start(s32[32]{0:T(128)} %param.17) | copy-start | bytes 388
  13.7 7.7 %copy-start.4 = (s32[4096]{0:T(1024)S(1)}, s32[4096]{0:T(1024)}, u32[]{:S(2)}) copy-start(s32[4096]{0:T(1024)} %param.18) | copy-start | bytes 49156
  13.7 128.3 %all-to-all-start = ((bf16[16,256,768]{2,1,0:T(8,128)(2,1)}), bf16[16,256,768]{2,1,0:T(8,128)(2,1)}, u32[]{:S(2)}, u32[]{:S(2)}) async-start(bf16[16,256,768]{2,1,0:T(8,128)(2,1)} %stack.12), calls=%async_computation | async-start | bytes 12582912 | tf_op jit(solution)/shard_map/all_to_all | solution.py:59
  21.3 282.2 %all-gather.4.cloned.1.call-start = ((), (), s32[]{:S(2)}) async-start(), calls=%async_computation.4 | async-start | bytes 6684672 | tf_op jit(solution)/shard_map/all_gather | solution.py:116
  133.2 8.8 %copy-start = (bf16[256,4096]{1,0:T(8,128)(2,1)S(1)}, bf16[256,4096]{1,0:T(8,128)(2,1)}, u32[]{:S(2)}) copy-start(bf16[256,4096]{1,0:T(8,128)(2,1)} %param.15) | copy-start | bytes 6291460
  152.8 15.6 %collective-permute-start = (bf16[256,2,2,128]{3,0,2,1:T(8,128)(2,1)S(1)}, bf16[256,2,2,128]{3,0,2,1:T(8,128)(2,1)}, u32[]{:S(2)}, u32[]{:S(2)}) collective-permute-start(bf16[256,2,2,128]{3,0,2,1:T(8,128)(2,1)S(1)} %copy.81), channel_id=1, source_target_pairs={{0,64},{16,80},{32,96},{48,112},{64,128},{80,144},{96,160},{112,17... | collective-permute-start | bytes 786440 | tf_op jit(solution)/shard_map/ppermute | solution.py:14
  155.4 14.7 %collective-permute-start.1 = (bf16[256,2,2,128]{3,0,2,1:T(8,128)(2,1)S(1)}, bf16[256,2,2,128]{3,0,2,1:T(8,128)(2,1)}, u32[]{:S(2)}, u32[]{:S(2)}) collective-permute-start(bf16[256,2,2,128]{3,0,2,1:T(8,128)(2,1)S(1)} %copy.81), channel_id=1, source_target_pairs={{0,48},{16,64},{32,80},{48,96},{64,112},{80,128},{96,144},{112,160... | collective-permute-start | bytes 786440 | tf_op jit(solution)/shard_map/ppermute | solution.py:14
  162.0 15.9 %collective-permute-start.2 = (bf16[256,2,2,128]{3,0,2,1:T(8,128)(2,1)S(1)}, bf16[256,2,2,128]{3,0,2,1:T(8,128)(2,1)}, u32[]{:S(2)}, u32[]{:S(2)}) collective-permute-start(bf16[256,2,2,128]{3,0,2,1:T(8,128)(2,1)S(1)} %copy.81), channel_id=1, source_target_pairs={{0,32},{16,48},{32,64},{48,80},{64,96},{80,112},{96,128},{112,144}... | collective-permute-start | bytes 786440 | tf_op jit(solution)/shard_map/ppermute | solution.py:14
  166.3 14.0 %collective-permute-start.3 = (bf16[256,2,2,128]{3,0,2,1:T(8,128)(2,1)S(1)}, bf16[256,2,2,128]{3,0,2,1:T(8,128)(2,1)S(1)}, u32[]{:S(2)}, u32[]{:S(2)}) collective-permute-start(bf16[256,2,2,128]{3,0,2,1:T(8,128)(2,1)S(1)} %copy.81), channel_id=1, source_target_pairs={{0,16},{16,32},{32,48},{48,64},{64,80},{80,96},{96,112},{112,128},... | collective-permute-start | bytes 786440 | tf_op jit(solution)/shard_map/ppermute | solution.py:14
  181.8 4.0 %copy-start.3 = (bf16[256,256]{0,1:T(8,128)(2,1)S(1)}, bf16[256,256]{0,1:T(8,128)(2,1)}, u32[]{:S(2)}) copy-start(bf16[256,256]{0,1:T(8,128)(2,1)} %copy.83) | copy-start | bytes 393220
  185.8 2.7 copy-start.2
  190.1 13.8 %collective-permute-start.7 = (bf16[256,2,2,128]{0,3,2,1:T(8,128)(2,1)S(1)}, bf16[256,2,2,128]{0,3,2,1:T(8,128)(2,1)S(1)}, u32[]{:S(2)}, u32[]{:S(2)}) collective-permute-start(bf16[256,2,2,128]{0,3,2,1:T(8,128)(2,1)S(1)} %get-tuple-element.258), channel_id=1, source_target_pairs={{64,0},{80,16},{96,32},{112,48},{128,64},{144,80},{160,96},{176,11... | collective-permute-start | bytes 786440 | tf_op jit(solution)/shard_map/ppermute | solution.py:14
  193.8 12.4 %collective-permute-start.6 = (bf16[256,2,2,128]{0,3,2,1:T(8,128)(2,1)S(1)}, bf16[256,2,2,128]{0,3,2,1:T(8,128)(2,1)S(1)}, u32[]{:S(2)}, u32[]{:S(2)}) collective-permute-start(bf16[256,2,2,128]{0,3,2,1:T(8,128)(2,1)S(1)} %get-tuple-element.259), channel_id=1, source_target_pairs={{48,0},{64,16},{80,32},{96,48},{112,64},{128,80},{144,96},{160,112... | collective-permute-start | bytes 786440 | tf_op jit(solution)/shard_map/ppermute | solution.py:14
  195.7 13.5 %collective-permute-start.5 = (bf16[256,2,2,128]{0,3,2,1:T(8,128)(2,1)S(1)}, bf16[256,2,2,128]{0,3,2,1:T(8,128)(2,1)S(1)}, u32[]{:S(2)}, u32[]{:S(2)}) collective-permute-start(bf16[256,2,2,128]{0,3,2,1:T(8,128)(2,1)S(1)} %get-tuple-element.260), channel_id=1, source_target_pairs={{32,0},{48,16},{64,32},{80,48},{96,64},{112,80},{128,96},{144,112}... | collective-permute-start | bytes 786440 | tf_op jit(solution)/shard_map/ppermute | solution.py:14
  197.6 14.4 %collective-permute-start.4 = (bf16[256,2,2,128]{0,3,2,1:T(8,128)(2,1)S(1)}, bf16[256,2,2,128]{0,3,2,1:T(8,128)(2,1)S(1)}, u32[]{:S(2)}, u32[]{:S(2)}) collective-permute-start(bf16[256,2,2,128]{0,3,2,1:T(8,128)(2,1)S(1)} %get-tuple-element.257), channel_id=1, source_target_pairs={{16,0},{32,16},{48,32},{64,48},{80,64},{96,80},{112,96},{128,112},... | collective-permute-start | bytes 786440 | tf_op jit(solution)/shard_map/ppermute | solution.py:14
  215.5 38.8 %all-to-all-start.1 = ((bf16[256,16,256]{0,2,1:T(8,128)(2,1)}), bf16[256,16,256]{0,2,1:T(8,128)(2,1)}, u32[]{:S(2)}, u32[]{:S(2)}) async-start(bf16[256,16,256]{0,2,1:T(8,128)(2,1)} %bitcast.115), calls=%async_computation.2 | async-start | bytes 4194304 | tf_op jit(solution)/shard_map/all_to_all | solution.py:55
  223.2 158.1 %reduce-scatter.2.cloned.1.call-start = ((), (), s32[]{:S(2)}) async-start(), calls=%async_computation.3 | async-start | bytes 2228224 | tf_op jit(solution)/shard_map/reduce_scatter | solution.py:141
  258.2 3.4 copy-start.1
Sparse Core Ops, SparseCore 0:
  11.1 122.0 all-gather.5
  213.1 90.3 all-gather.3
  306.6 74.6 reduce-scatter.1
